TPU v7x, 128 devices: a whole 4x4x4 slice. The times are simulated.
128 devices in a mesh: ctx: 32 (over z, y_hi, x), ch: 4 (over y_lo, core).
Axes of the slice: x: 4, y: 4 (y_hi: 2, y_lo: 2; y = y_hi * 2 + y_lo), z: 4, core: 2. Of those that a mesh axis runs over, the one named last changes fastest.
Arguments:
- q_conv: bfloat16 [7168, 4096], P('ctx', 'ch'), may hold values from -6 to 6
- k_conv: bfloat16 [7168, 4096], P('ctx', 'ch'), may hold values from -6 to 6
- v_conv: bfloat16 [7168, 4096], P('ctx', 'ch'), may hold values from -6 to 6
- conv_filter: bfloat16 [7168, 256], P('ctx', 'ch'), may hold values from -1 to 1
- q_attn: bfloat16 [7168, 4096], P('ctx', 'ch'), may hold values from -5 to 5
- k_attn: bfloat16 [7168, 4096], P('ctx', 'ch'), may hold values from -5 to 5
- v_attn: bfloat16 [7168, 4096], P('ctx', 'ch'), may hold values from -6 to 6
- w_conv_out: bfloat16 [4096, 4096], P('ch'), may hold values from -0.09375 to 0.09375
- w_attn_out: bfloat16 [4096, 4096], P('ch'), may hold values from -0.375 to 0.375
Outputs:
- layer_out: bfloat16 [7168, 4096], P(('ctx', 'ch'))
All inputs are finite; a program needn't handle non-finite values.
Results may differ from a plain program's by a relative error of at most 0.018.
Values may be sent and summed in bfloat16 or wider, within the bound.
No kernel may reach another device: no remote copies, remote signals or barrier semaphores. Data moves between devices by JAX's collectives and lax.ppermute only.
A program may use at most 192 MiB of HBM per device.

v0:
```python
from functools import partial
import math
import jax
import jax.numpy as jnp
from jax import lax
from jax.sharding import PartitionSpec as P

HD = 128
two_pi = 2.0 * math.pi
neg_large = -1e30
highest = lax.Precision.HIGHEST


def angle_table(left_idx, right_idx, period):
    product = left_idx[:, None] * right_idx[None, :] % period
    return product.astype(jnp.float32) * (two_pi / period)


def section_coarse(values, cos_table, sin_table, twiddle):
    real_part = jnp.einsum("kn,nsc->ksc", cos_table, values, precision=highest)
    imag_part = -jnp.einsum("kn,nsc->ksc", sin_table, values, precision=highest)
    cos_twist = jnp.cos(twiddle)[:, :, None]
    sin_twist = jnp.sin(twiddle)[:, :, None]
    return (
        real_part * cos_twist + imag_part * sin_twist,
        imag_part * cos_twist - real_part * sin_twist,
    )


def section_fine(real_part, imag_part, cos_table, sin_table, direction):
    cos_real = jnp.einsum("kn,anc->akc", cos_table, real_part, precision=highest)
    cos_imag = jnp.einsum("kn,anc->akc", cos_table, imag_part, precision=highest)
    sin_real = jnp.einsum("kn,anc->akc", sin_table, real_part, precision=highest)
    sin_imag = jnp.einsum("kn,anc->akc", sin_table, imag_part, precision=highest)
    return (cos_real - direction * sin_imag, cos_imag + direction * sin_real)


def spectral_conv(gated, filters, my_index, tok_rows, count_ctx):
    chans = gated.shape[1]
    groups = filters.shape[1]
    share = chans // groups
    sub_rows = tok_rows // count_ctx
    period = 2 * count_ctx * tok_rows
    got_source, got_filter = (
        lax.all_to_all(
            gated.reshape(1, tok_rows, chans), "ctx", split_axis=1, concat_axis=0, tiled=True
        ),
        lax.all_to_all(
            filters.reshape(1, tok_rows, groups), "ctx", split_axis=1, concat_axis=0, tiled=True
        ),
    )
    coarse_idx = jnp.arange(count_ctx, dtype=jnp.int32)
    coarse_freq = jnp.arange(2 * count_ctx, dtype=jnp.int32)
    coarse_angle = angle_table(coarse_freq, coarse_idx, 2 * count_ctx)
    cos_coarse = jnp.cos(coarse_angle)
    sin_coarse = jnp.sin(coarse_angle)
    fine_global = my_index * sub_rows + jnp.arange(sub_rows, dtype=jnp.int32)
    twist_in = angle_table(coarse_freq, fine_global, period)
    source_re, source_im = section_coarse(
        got_source.astype(jnp.float32), cos_coarse, sin_coarse, twist_in
    )
    filter_re, filter_im = section_coarse(
        got_filter.astype(jnp.float32), cos_coarse, sin_coarse, twist_in
    )
    source_re, source_im, filter_re, filter_im = (
        lax.all_to_all(
            source_re.astype(jnp.bfloat16), "ctx", split_axis=0, concat_axis=1, tiled=True
        ).astype(source_re.dtype),
        lax.all_to_all(
            source_im.astype(jnp.bfloat16), "ctx", split_axis=0, concat_axis=1, tiled=True
        ).astype(source_im.dtype),
        lax.all_to_all(
            filter_re.astype(jnp.bfloat16), "ctx", split_axis=0, concat_axis=1, tiled=True
        ).astype(filter_re.dtype),
        lax.all_to_all(
            filter_im.astype(jnp.bfloat16), "ctx", split_axis=0, concat_axis=1, tiled=True
        ).astype(filter_im.dtype),
    )
    fine_idx = jnp.arange(tok_rows, dtype=jnp.int32)
    fine_angle = angle_table(fine_idx, fine_idx, tok_rows)
    cos_fine = jnp.cos(fine_angle)
    sin_fine = jnp.sin(fine_angle)
    source_re, source_im = section_fine(source_re, source_im, cos_fine, sin_fine, -1.0)
    filter_re, filter_im = section_fine(filter_re, filter_im, cos_fine, sin_fine, -1.0)
    split_re = source_re.reshape(2, tok_rows, groups, share)
    split_im = source_im.reshape(2, tok_rows, groups, share)
    prod_re = split_re * filter_re[..., None] - split_im * filter_im[..., None]
    prod_im = split_re * filter_im[..., None] + split_im * filter_re[..., None]
    back_re, back_im = section_fine(
        prod_re.reshape(2, tok_rows, chans),
        prod_im.reshape(2, tok_rows, chans),
        cos_fine,
        sin_fine,
        1.0,
    )
    pair_freq = my_index * 2 + jnp.arange(2, dtype=jnp.int32)
    twist_out = angle_table(pair_freq, fine_idx, period)
    cos_out = jnp.cos(twist_out)[:, :, None]
    sin_out = jnp.sin(twist_out)[:, :, None]
    turned_re = back_re * cos_out - back_im * sin_out
    turned_im = back_re * sin_out + back_im * cos_out
    turned_re, turned_im = (
        lax.all_to_all(
            turned_re.astype(jnp.bfloat16), "ctx", split_axis=1, concat_axis=0, tiled=True
        ).astype(turned_re.dtype),
        lax.all_to_all(
            turned_im.astype(jnp.bfloat16), "ctx", split_axis=1, concat_axis=0, tiled=True
        ).astype(turned_im.dtype),
    )
    result = jnp.einsum("nk,ksc->nsc", cos_coarse.T, turned_re, precision=highest)
    result = result - jnp.einsum("nk,ksc->nsc", sin_coarse.T, turned_im, precision=highest)
    rounded = (result / period).astype(jnp.bfloat16)
    returned = lax.all_to_all(rounded, "ctx", split_axis=0, concat_axis=1, tiled=True)
    return returned.reshape(tok_rows, chans)


def keep_same(running):
    return running


def attend_block(group_query, group_pos, key_block, value_block, key_pos, score_scale, group_state):
    run_max, run_total, run_accum = group_state
    scores = (
        jnp.einsum("thd,shd->hts", group_query, key_block, preferred_element_type=jnp.float32)
        * score_scale
    )
    allowed = (key_pos[None, :] <= group_pos[:, None])[None]
    block_max = jnp.max(jnp.where(allowed, scores, neg_large), axis=2)
    new_max = jnp.maximum(run_max, block_max)
    factor = jnp.exp(run_max - new_max)
    weights = jnp.where(allowed, jnp.exp(scores - new_max[:, :, None]), 0.0)
    new_total = run_total * factor + jnp.sum(weights, axis=2)
    new_accum = run_accum * factor[:, :, None] + jnp.einsum(
        "hts,shd->htd",
        weights.astype(jnp.bfloat16),
        value_block,
        preferred_element_type=jnp.float32,
    )
    return (new_max, new_total, new_accum)


def attention(q_attn, k_attn, v_attn, my_index, tok_rows):
    heads_local = q_attn.shape[1] // HD
    score_scale = HD ** (-0.5)
    queries = q_attn.reshape(tok_rows, heads_local, HD)
    group_list = [(queries, my_index * tok_rows + jnp.arange(tok_rows, dtype=jnp.int32))]
    initial = tuple(
        (
            (
                jnp.full((heads_local, entry[0].shape[0]), neg_large, jnp.float32),
                jnp.zeros((heads_local, entry[0].shape[0]), jnp.float32),
                jnp.zeros((heads_local, entry[0].shape[0], HD), jnp.float32),
            )
            for entry in group_list
        )
    )
    key_piece = lax.all_gather(k_attn, "ctx", axis=0, tiled=True)
    value_piece = lax.all_gather(v_attn, "ctx", axis=0, tiled=True)
    count_blocks = key_piece.shape[0] // tok_rows
    keys_split = key_piece.reshape(count_blocks, tok_rows, heads_local, HD)
    values_split = value_piece.reshape(count_blocks, tok_rows, heads_local, HD)

    def one_block(carry, item):
        key_block, value_block, block_number = item
        block_first = block_number * tok_rows
        key_pos = block_first + jnp.arange(tok_rows, dtype=jnp.int32)
        updated = []
        for entry, group_state in zip(group_list, carry):
            step_fn = partial(
                attend_block, entry[0], entry[1], key_block, value_block, key_pos, score_scale
            )
            updated.append(lax.cond(block_first <= entry[1][-1], step_fn, keep_same, group_state))
        return (tuple(updated), None)

    new_state, unused = lax.scan(
        one_block, initial, (keys_split, values_split, jnp.arange(count_blocks, dtype=jnp.int32))
    )
    outputs = [
        (state[2] / state[1][:, :, None]).transpose(1, 0, 2).astype(jnp.bfloat16)
        for state in new_state
    ]
    merged = outputs[0]
    return merged.reshape(tok_rows, heads_local * HD)


def local(q_conv, k_conv, v_conv, conv_filter, q_attn, k_attn, v_attn, w_conv_out, w_attn_out):
    count_ctx = lax.axis_size("ctx")
    my_index = lax.axis_index("ctx")
    tok_rows = q_conv.shape[0]
    gated = (k_conv.astype(jnp.float32) * v_conv.astype(jnp.float32)).astype(jnp.bfloat16)
    conv = spectral_conv(gated, conv_filter, my_index, tok_rows, count_ctx)
    mixed = (q_conv.astype(jnp.float32) * conv.astype(jnp.float32)).astype(jnp.bfloat16)
    attended = attention(q_attn, k_attn, v_attn, my_index, tok_rows)
    return lax.psum_scatter(
        (
            jnp.dot(mixed, w_conv_out, preferred_element_type=jnp.float32)
            + jnp.dot(attended, w_attn_out, preferred_element_type=jnp.float32)
        ).astype(jnp.bfloat16),
        "ch",
        scatter_dimension=0,
        tiled=True,
    )


def solution(mesh):
    return jax.shard_map(
        local,
        mesh=mesh,
        in_specs=(
            P("ctx", "ch"),
            P("ctx", "ch"),
            P("ctx", "ch"),
            P("ctx", "ch"),
            P("ctx", "ch"),
            P("ctx", "ch"),
            P("ctx", "ch"),
            P("ch", None),
            P("ch", None),
        ),
        out_specs=P(("ctx", "ch"), None),
        check_vma=False,
    )
```

profile of v0, /device:TPU:1, one launch (start us, length us, event | category | flops | bytes accessed | tf_op | source)
XLA Modules:
  0.0 611.6 jit_solution(7817200553837334792)
XLA Ops:
  11.1 11.3 %all-to-all-start.3 = ((bf16[32,2,224]{2,1,0:T(2,128)(2,1)}), bf16[32,2,224]{2,1,0:T(2,128)(2,1)S(1)}, u32[]{:S(2)}, u32[]{:S(2)}) async-start(bf16[32,2,224]{2,1,0:T(2,128)(2,1)} %reshape.188), calls=%async_computation.3 | async-start | bytes 65536 | tf_op jit(solution)/shard_map/all_to_all | solution.py:48
  24.6 3.3 reduce.5
  29.0 2.2 all-to-all-done.3
  31.3 7.0 %all-to-all-start = ((bf16[32,2,3584]{2,1,0:T(2,128)(2,1)}), bf16[32,2,3584]{2,1,0:T(2,128)(2,1)S(1)}, u32[]{:S(2)}, u32[]{:S(2)}) async-start(bf16[32,2,3584]{2,1,0:T(2,128)(2,1)} %reshape.194), calls=%async_computation | async-start | bytes 917504 | tf_op jit(solution)/shard_map/all_to_all | solution.py:45
  41.2 7.5 %all-to-all-done = bf16[32,2,3584]{2,1,0:T(2,128)(2,1)S(1)} async-done(((bf16[32,2,3584]{2,1,0:T(2,128)(2,1)}), bf16[32,2,3584]{2,1,0:T(2,128)(2,1)S(1)}, u32[]{:S(2)}, u32[]{:S(2)}) %all-to-all-start) | async-done | bytes 458784 | tf_op jit(solution)/shard_map/all_to_all | solution.py:45
  48.7 4.4 all-to-all-start.5
  53.5 2.6 bitcast_reduce_fusion
  57.7 5.0 all-to-all-done.5
  62.7 4.3 all-to-all-start.4
  67.0 2.6 add_convert_fusion.1
  69.7 1.6 copy.89
  71.2 5.3 all-to-all-done.4
  76.5 4.1 all-to-all-start.1
  83.0 19.3 %all-to-all-done.1 = bf16[64,7,1024]{2,1,0:T(8,128)(2,1)S(1)} async-done(((bf16[64,7,1024]{2,1,0:T(8,128)(2,1)}), bf16[64,7,1024]{2,1,0:T(8,128)(2,1)S(1)}, u32[]{:S(2)}, u32[]{:S(2)}) %all-to-all-start.1) | async-done | bytes 917536 | tf_op jit(solution)/shard_map/all_to_all | solution.py:66
  102.2 5.0 all-to-all-start.2
  109.8 1.8 copy.104
  114.1 2.2 copy.109
  116.3 2.3 copy.90
  118.6 6.3 %all-to-all-done.2 = bf16[64,7,1024]{2,1,0:T(8,128)(2,1)} async-done(((bf16[64,7,1024]{2,1,0:T(8,128)(2,1)}), bf16[64,7,1024]{2,1,0:T(8,128)(2,1)}, u32[]{:S(2)}, u32[]{:S(2)}) %all-to-all-start.2) | async-done | bytes 917536 | tf_op jit(solution)/shard_map/all_to_all | solution.py:69
  124.9 2.3 copy.93
  127.1 1.8 fusion.30
  129.0 1.8 fusion.34
  130.8 2.0 multiply_subtract_fusion
  132.9 2.5 fusion.20
  135.4 2.9 fusion.55
  138.2 2.7 fusion.53
  140.9 2.7 convolution_add_fusion.2
  143.6 3.8 fusion.29
  147.4 1.9 copy.114
  149.3 4.2 all-to-all-start.7
  153.5 1.9 copy.112
  155.4 10.4 %all-to-all-done.7 = bf16[2,224,1024]{2,0,1:T(2,128)(2,1)S(1)} async-done(((bf16[2,224,1024]{2,0,1:T(2,128)(2,1)}), bf16[2,224,1024]{2,0,1:T(2,128)(2,1)S(1)}, u32[]{:S(2)}, u32[]{:S(2)}) %all-to-all-start.7) | async-done | bytes 917536 | tf_op jit(solution)/shard_map/all_to_all | solution.py:106
  165.8 6.0 all-to-all-start.6
  172.7 19.2 %all-to-all-done.6 = bf16[2,224,1024]{2,0,1:T(2,128)(2,1)S(1)} async-done(((bf16[2,224,1024]{2,0,1:T(2,128)(2,1)}), bf16[2,224,1024]{2,0,1:T(2,128)(2,1)S(1)}, u32[]{:S(2)}, u32[]{:S(2)}) %all-to-all-start.6) | async-done | bytes 917536 | tf_op jit(solution)/shard_map/all_to_all | solution.py:103
  195.3 5.5 all-to-all-start.8
  201.0 10.9 %all-to-all-done.8 = bf16[32,7,1024]{2,1,0:T(8,128)(2,1)S(1)} async-done(((bf16[32,7,1024]{2,1,0:T(8,128)(2,1)}), bf16[32,7,1024]{2,1,0:T(8,128)(2,1)S(1)}, u32[]{:S(2)}, u32[]{:S(2)}) %all-to-all-start.8) | async-done | bytes 458784 | tf_op jit(solution)/shard_map/all_to_all | solution.py:113
  212.0 7.3 %fusion.37 = f32[224,4096]{1,0:T(8,128)} fusion(bf16[1024,4096]{1,0:T(8,128)(2,1)} %param.20, f32[224,1024]{1,0:T(8,128)S(1)} %reshape.181, bf16[224,1024]{1,0:T(8,128)(2,1)S(1)} %copy-done.6), kind=kOutput, calls=%fused_computation.63 | convolution fusion | flops 1879736320 | bytes 13434880 | tf_op jit(solution)/shard_map/dot_general | solution.py:196
  219.3 9.2 %copy.126 = bf16[896,8,8,128]{3,2,1,0:T(8,128)(2,1)S(1)} copy(bf16[896,8,8,128]{3,1,2,0:T(8,128)(2,1)} %bitcast.171) | data formatting | bytes 29360128
  228.6 7.3 %copy.117 = bf16[32,224,8,128]{3,1,2,0:T(8,128)(2,1)} copy(bf16[32,224,8,128]{3,2,1,0:T(8,128)(2,1)S(1)} %bitcast.169) | data formatting | bytes 29360128 | tf_op jit(solution)/shard_map/while | solution.py:175
  235.9 97.1 %all-gather.5.cloned.1.call-done = bf16[7168,1024]{1,0:T(8,128)(2,1)} async-done(((bf16[224,1024]{1,0:T(8,128)(2,1)}), bf16[7168,1024]{1,0:T(8,128)(2,1)}) %all-gather.5.cloned.1.call-update) | async-done | bytes 14680080 | tf_op jit(solution)/shard_map/all_gather | solution.py:158
  333.0 9.1 %copy.127 = bf16[896,8,8,128]{3,2,1,0:T(8,128)(2,1)S(1)} copy(bf16[896,8,8,128]{3,1,2,0:T(8,128)(2,1)} %bitcast.172) | data formatting | bytes 29360128
  342.1 7.3 %copy.119 = bf16[32,224,8,128]{3,1,2,0:T(8,128)(2,1)} copy(bf16[32,224,8,128]{3,2,1,0:T(8,128)(2,1)S(1)} %bitcast.170) | data formatting | bytes 29360128 | tf_op jit(solution)/shard_map/while | solution.py:175
  349.5 92.0 %while.14 = (s32[]{:T(128)}, f32[8,224]{1,0:T(8,128)S(1)}, f32[8,224]{1,0:T(8,128)S(1)}, f32[8,224,128]{2,1,0:T(8,128)S(1)}, s32[32]{0:T(128)S(1)}, /*index=5*/s...) while((s32[]{:T(128)}, f32[8,224]{1,0:T(8,128)S(1)}, ...), condition=%wide.region_5.6_spmd, body=%wide.region_0.5_spmd.sunk | while | flops 210449120 | bytes 8349359 | solution.py:175
  352.2 4.2 conditional.2
  352.4 1.5 fusion
  354.3 2.1 convolution_add_fusion
  441.5 7.9 %fusion.19 = bf16[224,4096]{1,0:T(8,128)(2,1)} fusion(f32[224,4096]{1,0:T(8,128)} %fusion.37, bf16[1024,4096]{1,0:T(8,128)(2,1)} %param.21, f32[8,224,128]{2,1,0:T(8,128)S(1)} %get-tuple-element.145, f32[8,224]{1,0:T(8,128)S(1)} %get-tuple-element.146), kind=kOutput, calls=%fused_computation.26 | convolution fusion | flops 1881341952 | bytes 14818304 | tf_op jit(solution)/shard_map/dot_general | solution.py:197
  449.4 155.4 %reduce-scatter.2.cloned.1.call-done = bf16[56,4096]{1,0:T(8,128)(2,1)} async-done(((bf16[224,4096]{1,0:T(8,128)(2,1)}), bf16[56,4096]{1,0:T(8,128)(2,1)}) %reduce-scatter.2.cloned.1.call-update) | async-done | bytes 458768 | tf_op jit(solution)/shard_map/reduce_scatter | solution.py:194
  (204 shorter events, 67.8 us)
Async XLA Ops:
  6.5 194.3 %copy-start = (bf16[224,1024]{1,0:T(8,128)(2,1)S(1)}, bf16[224,1024]{1,0:T(8,128)(2,1)}, u32[]{:S(2)}) copy-start(bf16[224,1024]{1,0:T(8,128)(2,1)} %param.17) | copy-start | bytes 1376260
  6.5 212.8 %all-gather.3.cloned.1.call-start = ((), (), s32[]{:S(2)}) async-start(), calls=%async_computation.10 | async-start | bytes 15138816 | tf_op jit(solution)/shard_map/all_gather | solution.py:157
  7.3 325.7 %all-gather.5.cloned.1.call-start = ((), (), s32[]{:S(2)}) async-start(), calls=%async_computation.11 | async-start | bytes 15138816 | tf_op jit(solution)/shard_map/all_gather | solution.py:158
  11.1 20.2 %all-to-all-start.3 = ((bf16[32,2,224]{2,1,0:T(2,128)(2,1)}), bf16[32,2,224]{2,1,0:T(2,128)(2,1)S(1)}, u32[]{:S(2)}, u32[]{:S(2)}) async-start(bf16[32,2,224]{2,1,0:T(2,128)(2,1)} %reshape.188), calls=%async_computation.3 | async-start | bytes 65536 | tf_op jit(solution)/shard_map/all_to_all | solution.py:48
  31.3 17.5 %all-to-all-start = ((bf16[32,2,3584]{2,1,0:T(2,128)(2,1)}), bf16[32,2,3584]{2,1,0:T(2,128)(2,1)S(1)}, u32[]{:S(2)}, u32[]{:S(2)}) async-start(bf16[32,2,3584]{2,1,0:T(2,128)(2,1)} %reshape.194), calls=%async_computation | async-start | bytes 917504 | tf_op jit(solution)/shard_map/all_to_all | solution.py:45
  48.7 14.0 %all-to-all-start.5 = ((bf16[32,2,448]{2,1,0:T(2,128)(2,1)}), bf16[32,2,448]{2,1,0:T(2,128)(2,1)S(1)}, u32[]{:S(2)}, u32[]{:S(2)}) async-start(bf16[32,2,448]{2,1,0:T(2,128)(2,1)} %reshape.192), calls=%async_computation.5 | async-start | bytes 131072 | tf_op jit(solution)/shard_map/all_to_all | solution.py:75
  62.7 13.8 %all-to-all-start.4 = ((bf16[32,2,448]{2,1,0:T(2,128)(2,1)}), bf16[32,2,448]{2,1,0:T(2,128)(2,1)S(1)}, u32[]{:S(2)}, u32[]{:S(2)}) async-start(bf16[32,2,448]{2,1,0:T(2,128)(2,1)} %reshape.190), calls=%async_computation.4 | async-start | bytes 131072 | tf_op jit(solution)/shard_map/all_to_all | solution.py:72
  71.2 10.2 %copy-start.5 = (bf16[64,7,1024]{2,0,1:T(8,128)(2,1)S(1)}, bf16[64,7,1024]{2,0,1:T(8,128)(2,1)}, u32[]{:S(2)}) copy-start(bf16[64,7,1024]{2,0,1:T(8,128)(2,1)} %get-tuple-element.199) | copy-start | bytes 2752516
  76.5 25.7 %all-to-all-start.1 = ((bf16[64,7,1024]{2,1,0:T(8,128)(2,1)}), bf16[64,7,1024]{2,1,0:T(8,128)(2,1)S(1)}, u32[]{:S(2)}, u32[]{:S(2)}) async-start(bf16[64,7,1024]{2,1,0:T(8,128)(2,1)} %copy.89), calls=%async_computation.1 | async-start | bytes 2097152 | tf_op jit(solution)/shard_map/all_to_all | solution.py:66
  102.2 6.2 %copy-start.4 = (bf16[64,7,1024]{2,1,0:T(8,128)(2,1)}, bf16[64,7,1024]{2,1,0:T(8,128)(2,1)S(1)}, u32[]{:S(2)}) copy-start(bf16[64,7,1024]{2,1,0:T(8,128)(2,1)S(1)} %all-to-all-done.1) | copy-start | bytes 2752516
  102.2 22.6 %all-to-all-start.2 = ((bf16[64,7,1024]{2,1,0:T(8,128)(2,1)}), bf16[64,7,1024]{2,1,0:T(8,128)(2,1)}, u32[]{:S(2)}, u32[]{:S(2)}) async-start(bf16[64,7,1024]{2,1,0:T(8,128)(2,1)} %copy.92), calls=%async_computation.2 | async-start | bytes 2097152 | tf_op jit(solution)/shard_map/all_to_all | solution.py:69
  130.8 2.0 copy-start.2
  130.8 2.0 copy-start.3
  149.3 16.5 %all-to-all-start.7 = ((bf16[2,224,1024]{2,0,1:T(2,128)(2,1)}), bf16[2,224,1024]{2,0,1:T(2,128)(2,1)S(1)}, u32[]{:S(2)}, u32[]{:S(2)}) async-start(bf16[2,224,1024]{2,0,1:T(2,128)(2,1)} %copy.114), calls=%async_computation.7 | async-start | bytes 1835008 | tf_op jit(solution)/shard_map/all_to_all | solution.py:106
  165.8 26.2 %all-to-all-start.6 = ((bf16[2,224,1024]{2,0,1:T(2,128)(2,1)}), bf16[2,224,1024]{2,0,1:T(2,128)(2,1)S(1)}, u32[]{:S(2)}, u32[]{:S(2)}) async-start(bf16[2,224,1024]{2,0,1:T(2,128)(2,1)} %copy.112), calls=%async_computation.6 | async-start | bytes 1835008 | tf_op jit(solution)/shard_map/all_to_all | solution.py:103
  195.3 16.7 %copy-start.6 = (bf16[224,1024]{1,0:T(8,128)(2,1)S(1)}, bf16[224,1024]{1,0:T(8,128)(2,1)}, u32[]{:S(2)}) copy-start(bf16[224,1024]{1,0:T(8,128)(2,1)} %param.13) | copy-start | bytes 1376260
  195.3 16.6 %all-to-all-start.8 = ((bf16[32,7,1024]{2,1,0:T(8,128)(2,1)}), bf16[32,7,1024]{2,1,0:T(8,128)(2,1)S(1)}, u32[]{:S(2)}, u32[]{:S(2)}) async-start(bf16[32,7,1024]{2,1,0:T(8,128)(2,1)} %copy.116), calls=%async_computation.8 | async-start | bytes 1048576 | tf_op jit(solution)/shard_map/all_to_all | solution.py:113
  200.8 404.0 %reduce-scatter.2.cloned.1.call-start = ((), (), s32[]{:S(2)}) async-start(), calls=%async_computation.12 | async-start | bytes 2293760 | tf_op jit(solution)/shard_map/reduce_scatter | solution.py:194
  441.5 163.3 %copy-start.1 = (bf16[224,1024]{1,0:T(8,128)(2,1)S(1)}, bf16[224,1024]{1,0:T(8,128)(2,1)}, u32[]{:S(2)}) copy-start(bf16[224,1024]{1,0:T(8,128)(2,1)} %param.17) | copy-start | bytes 1376260
Sparse Core Ops, SparseCore 0:
  10.4 179.5 all-gather.2
  193.1 139.8 all-gather.4
  449.5 155.2 reduce-scatter.1
where the time goes:
time: 622 us; the launch traced here: 612 us
  waiting for transfers between devices  340 us (55%)
  local copies, waits for them, and re-layouts  104 us (17%)
  starting transfers between devices  51.9 us (8%)
  matrix products  49.7 us (8%)
  loops' own time  45.7 us (7%)
  between operations  13.9 us (2%)
  other arithmetic  6.44 us (1%)
    reduce_scatter x1, waiting for transfers between devices, local(): lax.psum_scatter((jnp.dot(mixed, w_conv_out, preferred_element_type=jnp.f...  155 us
    all_gather x1, waiting for transfers between devices, attention(): value_piece = lax.all_gather(v_attn, 'ctx', axis=0, tiled=True)  97.1 us
    another operation x1, loops' own time, attention(): lax.scan(one_block, initial, (keys_split, values_split, jnp.arange(count_...  45.1 us
    unnamed x25, local copies, waits for them, and re-layouts  23 us
    dynamic_slice x32, local copies, waits for them, and re-layouts, attention(): lax.scan(one_block, initial, (keys_split, values_split, jnp.arange(count_...  21.2 us
    slice x32, local copies, waits for them, and re-layouts, one_block(): entry[1][-1]  20.8 us
    all_to_all x1, waiting for transfers between devices, spectral_conv(): lax.all_to_all(source_re.astype(jnp.bfloat16), 'ctx', split_axis=0, conca...  19.3 us
    all_to_all x1, waiting for transfers between devices, spectral_conv(): lax.all_to_all(turned_re.astype(jnp.bfloat16), 'ctx', split_axis=1, conca...  19.2 us
  transfers between devices with their start and end apart: 12, of which 11 were waited for; matrix products, arithmetic and copies ran while one was open for 14% of the time, Pallas kernels for 0%

commit v1 on v0

--- a/solution.py
+++ b/solution.py
@@ -155,7 +155,9 @@
         )
     )
     key_piece = lax.all_gather(k_attn, "ctx", axis=0, tiled=True)
-    value_piece = lax.all_gather(v_attn, "ctx", axis=0, tiled=True)
+    value_piece = jnp.concatenate(
+        lax.all_to_all(jnp.stack([v_attn] * lax.axis_size("ctx")), "ctx", 0, 0), axis=0
+    )
     count_blocks = key_piece.shape[0] // tok_rows
     keys_split = key_piece.reshape(count_blocks, tok_rows, heads_local, HD)
     values_split = value_piece.reshape(count_blocks, tok_rows, heads_local, HD)

time: 622 us -> 738 us (1.19)
  waiting for transfers between devices: 340 us -> 438 us
  blocking collectives: 0 us -> 16.6 us
    all_to_all x1, waiting for transfers between devices: 10.9 us -> 189 us  [attention(): lax.all_to_all(jnp.stack([v_attn] * lax.axis_size('ctx')), 'ctx', 0, 0)]
    all_gather x1 -> x0, waiting for transfers between devices: 97.1 us -> none  [attention(): value_piece = lax.all_gather(v_attn, 'ctx', axis=0, tiled=True)]
    reduce_scatter x1, waiting for transfers between devices: 155 us -> 175 us  [local(): lax.psum_scatter((jnp.dot(mixed, w_conv_out, preferred_element_type=jnp.f...]
    all_to_all x0 -> x1, blocking collectives: none -> 16.6 us  [spectral_conv(): lax.all_to_all(rounded, 'ctx', split_axis=0, concat_axis=1, tiled=True)]
    all_to_all x1, waiting for transfers between devices: 19.2 us -> 10.4 us  [spectral_conv(): lax.all_to_all(turned_re.astype(jnp.bfloat16), 'ctx', split_axis=1, conca...]
    unnamed x25 -> x26, local copies, waits for them, and re-layouts: 23 us -> 14.5 us
    all_to_all x1, waiting for transfers between devices: 10.4 us -> 17.8 us  [spectral_conv(): lax.all_to_all(turned_im.astype(jnp.bfloat16), 'ctx', split_axis=1, conca...]
  transfers between devices with their start and end apart: 12 -> 11, of which waited for: 11 -> 10; matrix products, arithmetic and copies ran while one was open for 14% -> 13% of each run, Pallas kernels for 0% -> 0%
where the time goes in v1:
time: 738 us; the launch traced here: 727 us
  waiting for transfers between devices  438 us (59%)
  local copies, waits for them, and re-layouts  107 us (14%)
  starting transfers between devices  51.6 us (7%)
  matrix products  49.8 us (7%)
  loops' own time  43 us (6%)
  blocking collectives  16.6 us (2%)
  between operations  14.2 us (2%)
    all_to_all x1, waiting for transfers between devices, attention(): lax.all_to_all(jnp.stack([v_attn] * lax.axis_size('ctx')), 'ctx', 0, 0)  189 us
    reduce_scatter x1, waiting for transfers between devices, local(): lax.psum_scatter((jnp.dot(mixed, w_conv_out, preferred_element_type=jnp.f...  175 us
    another operation x1, loops' own time, attention(): lax.scan(one_block, initial, (keys_split, values_split, jnp.arange(count_...  42.6 us
    while x3, local copies, waits for them, and re-layouts, attention(): lax.scan(one_block, initial, (keys_split, values_split, jnp.arange(count_...  21.8 us
    dynamic_slice x32, local copies, waits for them, and re-layouts, attention(): lax.scan(one_block, initial, (keys_split, values_split, jnp.arange(count_...  21 us
    slice x32, local copies, waits for them, and re-layouts, one_block(): entry[1][-1]  19.6 us
    all_to_all x1, waiting for transfers between devices, spectral_conv(): lax.all_to_all(turned_im.astype(jnp.bfloat16), 'ctx', split_axis=1, conca...  17.8 us
    all_to_all x1, waiting for transfers between devices, spectral_conv(): lax.all_to_all(source_re.astype(jnp.bfloat16), 'ctx', split_axis=0, conca...  17.3 us
  transfers between devices with their start and end apart: 11, of which 10 were waited for; matrix products, arithmetic and copies ran while one was open for 13% of the time, Pallas kernels for 0%

profile of v1, /device:TPU:1, one launch (start us, length us, event | category | flops | bytes accessed | tf_op | source)
XLA Modules:
  0.0 727.3 jit_solution(17675321367677039023)
XLA Ops:
  10.3 11.3 %all-to-all-start.3 = ((bf16[32,2,224]{2,1,0:T(2,128)(2,1)}), bf16[32,2,224]{2,1,0:T(2,128)(2,1)S(1)}, u32[]{:S(2)}, u32[]{:S(2)}) async-start(bf16[32,2,224]{2,1,0:T(2,128)(2,1)} %reshape.186), calls=%async_computation.3 | async-start | bytes 65536 | tf_op jit(solution)/shard_map/all_to_all | solution.py:48
  23.9 3.3 reduce.5
  28.2 2.2 all-to-all-done.3
  30.4 7.1 all-to-all-start
  40.5 7.5 %all-to-all-done = bf16[32,2,3584]{2,1,0:T(2,128)(2,1)S(1)} async-done(((bf16[32,2,3584]{2,1,0:T(2,128)(2,1)}), bf16[32,2,3584]{2,1,0:T(2,128)(2,1)S(1)}, u32[]{:S(2)}, u32[]{:S(2)}) %all-to-all-start) | async-done | bytes 458784 | tf_op jit(solution)/shard_map/all_to_all | solution.py:45
  48.0 4.5 all-to-all-start.4
  52.8 2.6 bitcast_reduce_fusion
  57.0 4.9 all-to-all-done.4
  61.9 4.4 all-to-all-start.5
  66.3 2.7 add_convert_fusion.1
  69.0 1.5 copy.89
  70.5 5.3 all-to-all-done.5
  75.8 4.1 all-to-all-start.1
  82.2 17.3 %all-to-all-done.1 = bf16[64,7,1024]{2,1,0:T(8,128)(2,1)S(1)} async-done(((bf16[64,7,1024]{2,1,0:T(8,128)(2,1)}), bf16[64,7,1024]{2,1,0:T(8,128)(2,1)S(1)}, u32[]{:S(2)}, u32[]{:S(2)}) %all-to-all-start.1) | async-done | bytes 917536 | tf_op jit(solution)/shard_map/all_to_all | solution.py:66
  99.6 5.1 all-to-all-start.2
  107.3 1.8 copy.104
  111.7 2.1 copy.109
  113.8 2.3 copy.90
  116.1 8.4 %all-to-all-done.2 = bf16[64,7,1024]{2,1,0:T(8,128)(2,1)} async-done(((bf16[64,7,1024]{2,1,0:T(8,128)(2,1)}), bf16[64,7,1024]{2,1,0:T(8,128)(2,1)}, u32[]{:S(2)}, u32[]{:S(2)}) %all-to-all-start.2) | async-done | bytes 917536 | tf_op jit(solution)/shard_map/all_to_all | solution.py:69
  124.5 2.3 copy.93
  126.8 1.8 fusion.34
  128.6 1.8 fusion.30
  130.5 2.0 multiply_subtract_fusion
  132.5 2.5 fusion.20
  135.0 2.9 fusion.53
  137.9 2.7 fusion.55
  140.5 2.7 convolution_add_fusion.2
  143.3 3.8 fusion.29
  147.0 1.9 copy.112
  148.9 4.6 all-to-all-start.6
  153.5 1.9 copy.114
  155.4 10.4 %all-to-all-done.6 = bf16[2,224,1024]{2,0,1:T(2,128)(2,1)S(1)} async-done(((bf16[2,224,1024]{2,0,1:T(2,128)(2,1)}), bf16[2,224,1024]{2,0,1:T(2,128)(2,1)S(1)}, u32[]{:S(2)}, u32[]{:S(2)}) %all-to-all-start.6) | async-done | bytes 917536 | tf_op jit(solution)/shard_map/all_to_all | solution.py:103
  165.8 5.3 all-to-all-start.7
  172.1 17.8 %all-to-all-done.7 = bf16[2,224,1024]{2,0,1:T(2,128)(2,1)S(1)} async-done(((bf16[2,224,1024]{2,0,1:T(2,128)(2,1)}), bf16[2,224,1024]{2,0,1:T(2,128)(2,1)S(1)}, u32[]{:S(2)}, u32[]{:S(2)}) %all-to-all-start.7) | async-done | bytes 917536 | tf_op jit(solution)/shard_map/all_to_all | solution.py:106
  192.4 16.6 %all_to_all.146 = bf16[32,7,1024]{2,1,0:T(8,128)(2,1)S(1)} all-to-all(bf16[32,7,1024]{2,1,0:T(8,128)(2,1)S(1)} %copy.116), channel_id=1, replica_groups=mesh['ctx'=32,'ch'=4] {'ctx'}, dimensions={0} | all-to-all | bytes 917504 | tf_op jit(solution)/shard_map/all_to_all | solution.py:113
  209.0 7.0 stack.2
  216.0 5.1 all-to-all-start.9
  222.2 7.4 %fusion.37 = f32[224,4096]{1,0:T(8,128)} fusion(bf16[1024,4096]{1,0:T(8,128)(2,1)} %param.20, f32[224,1024]{1,0:T(8,128)S(1)} %reshape.179, bf16[224,1024]{1,0:T(8,128)(2,1)S(1)} %copy-done.6), kind=kOutput, calls=%fused_computation.64 | convolution fusion | flops 1879736320 | bytes 13434880 | tf_op jit(solution)/shard_map/dot_general | solution.py:198
  229.5 189.1 %all-to-all-done.9 = bf16[32,224,1024]{2,1,0:T(8,128)(2,1)} async-done(((bf16[32,224,1024]{2,1,0:T(8,128)(2,1)}), bf16[32,224,1024]{2,1,0:T(8,128)(2,1)}, u32[]{:S(2)}, u32[]{:S(2)}) %all-to-all-start.9) | async-done | bytes 14680096 | tf_op jit(solution)/shard_map/all_to_all | solution.py:159
  418.7 14.3 %copy_bitcast_fusion = bf16[32,224,8,128]{3,1,2,0:T(8,128)(2,1)} fusion(bf16[32,224,1024]{2,1,0:T(8,128)(2,1)} %all-to-all-done.9), kind=kLoop, calls=%fused_computation.25 | loop fusion | bytes 29360128 | tf_op jit(solution)/shard_map/while | solution.py:177
  433.0 9.1 %copy.127 = bf16[896,8,8,128]{3,2,1,0:T(8,128)(2,1)S(1)} copy(bf16[896,8,8,128]{3,1,2,0:T(8,128)(2,1)} %bitcast.172) | data formatting | bytes 29360128
  442.1 7.4 %copy.117 = bf16[32,224,8,128]{3,1,2,0:T(8,128)(2,1)} copy(bf16[32,224,8,128]{3,2,1,0:T(8,128)(2,1)S(1)} %bitcast.171) | data formatting | bytes 29360128 | tf_op jit(solution)/shard_map/while | solution.py:177
  449.6 87.9 %while.14 = (s32[]{:T(128)}, f32[8,224]{1,0:T(8,128)S(1)}, f32[8,224]{1,0:T(8,128)S(1)}, f32[8,224,128]{2,1,0:T(8,128)S(1)}, s32[32]{0:T(128)S(1)}, /*index=5*/s...) while((s32[]{:T(128)}, f32[8,224]{1,0:T(8,128)S(1)}, ...), condition=%wide.region_5.6_spmd, body=%wide.region_0.5_spmd.sunk | while | flops 210449120 | bytes 8349351 | solution.py:177
  452.2 4.2 conditional.2
  452.3 1.5 fusion
  454.3 2.1 convolution_add_fusion
  537.5 7.9 %fusion.19 = bf16[224,4096]{1,0:T(8,128)(2,1)} fusion(f32[224,4096]{1,0:T(8,128)} %fusion.37, bf16[1024,4096]{1,0:T(8,128)(2,1)} %param.21, f32[8,224,128]{2,1,0:T(8,128)S(1)} %get-tuple-element.145, f32[8,224]{1,0:T(8,128)S(1)} %get-tuple-element.146), kind=kOutput, calls=%fused_computation.27 | convolution fusion | flops 1881341952 | bytes 14818304 | tf_op jit(solution)/shard_map/dot_general | solution.py:199
  545.4 174.8 %reduce-scatter.2.cloned.1.call-done = bf16[56,4096]{1,0:T(8,128)(2,1)} async-done(((bf16[224,4096]{1,0:T(8,128)(2,1)}), bf16[56,4096]{1,0:T(8,128)(2,1)}) %reduce-scatter.2.cloned.1.call-update) | async-done | bytes 458768 | tf_op jit(solution)/shard_map/reduce_scatter | solution.py:196
  (204 shorter events, 65.2 us)
Async XLA Ops:
  6.5 214.7 %copy-start = (bf16[224,1024]{1,0:T(8,128)(2,1)S(1)}, bf16[224,1024]{1,0:T(8,128)(2,1)}, u32[]{:S(2)}) copy-start(bf16[224,1024]{1,0:T(8,128)(2,1)} %param.17) | copy-start | bytes 1376260
  6.5 426.4 %all-gather.2.cloned.1.call-start = ((), (), s32[]{:S(2)}) async-start(), calls=%async_computation.11 | async-start | bytes 15138816 | tf_op jit(solution)/shard_map/all_gather | solution.py:157
  10.3 20.1 %all-to-all-start.3 = ((bf16[32,2,224]{2,1,0:T(2,128)(2,1)}), bf16[32,2,224]{2,1,0:T(2,128)(2,1)S(1)}, u32[]{:S(2)}, u32[]{:S(2)}) async-start(bf16[32,2,224]{2,1,0:T(2,128)(2,1)} %reshape.186), calls=%async_computation.3 | async-start | bytes 65536 | tf_op jit(solution)/shard_map/all_to_all | solution.py:48
  30.4 17.5 %all-to-all-start = ((bf16[32,2,3584]{2,1,0:T(2,128)(2,1)}), bf16[32,2,3584]{2,1,0:T(2,128)(2,1)S(1)}, u32[]{:S(2)}, u32[]{:S(2)}) async-start(bf16[32,2,3584]{2,1,0:T(2,128)(2,1)} %reshape.192), calls=%async_computation | async-start | bytes 917504 | tf_op jit(solution)/shard_map/all_to_all | solution.py:45
  48.0 13.9 %all-to-all-start.4 = ((bf16[32,2,448]{2,1,0:T(2,128)(2,1)}), bf16[32,2,448]{2,1,0:T(2,128)(2,1)S(1)}, u32[]{:S(2)}, u32[]{:S(2)}) async-start(bf16[32,2,448]{2,1,0:T(2,128)(2,1)} %reshape.188), calls=%async_computation.4 | async-start | bytes 131072 | tf_op jit(solution)/shard_map/all_to_all | solution.py:72
  61.9 13.9 %all-to-all-start.5 = ((bf16[32,2,448]{2,1,0:T(2,128)(2,1)}), bf16[32,2,448]{2,1,0:T(2,128)(2,1)S(1)}, u32[]{:S(2)}, u32[]{:S(2)}) async-start(bf16[32,2,448]{2,1,0:T(2,128)(2,1)} %reshape.190), calls=%async_computation.5 | async-start | bytes 131072 | tf_op jit(solution)/shard_map/all_to_all | solution.py:75
  70.5 10.2 %copy-start.5 = (bf16[64,7,1024]{2,0,1:T(8,128)(2,1)S(1)}, bf16[64,7,1024]{2,0,1:T(8,128)(2,1)}, u32[]{:S(2)}) copy-start(bf16[64,7,1024]{2,0,1:T(8,128)(2,1)} %get-tuple-element.199) | copy-start | bytes 2752516
  75.8 23.8 %all-to-all-start.1 = ((bf16[64,7,1024]{2,1,0:T(8,128)(2,1)}), bf16[64,7,1024]{2,1,0:T(8,128)(2,1)S(1)}, u32[]{:S(2)}, u32[]{:S(2)}) async-start(bf16[64,7,1024]{2,1,0:T(8,128)(2,1)} %copy.89), calls=%async_computation.1 | async-start | bytes 2097152 | tf_op jit(solution)/shard_map/all_to_all | solution.py:66
  99.6 6.3 copy-start.4
  99.6 24.9 %all-to-all-start.2 = ((bf16[64,7,1024]{2,1,0:T(8,128)(2,1)}), bf16[64,7,1024]{2,1,0:T(8,128)(2,1)}, u32[]{:S(2)}, u32[]{:S(2)}) async-start(bf16[64,7,1024]{2,1,0:T(8,128)(2,1)} %copy.92), calls=%async_computation.2 | async-start | bytes 2097152 | tf_op jit(solution)/shard_map/all_to_all | solution.py:69
  130.5 2.0 copy-start.2
  130.5 2.0 copy-start.3
  148.9 16.9 %all-to-all-start.6 = ((bf16[2,224,1024]{2,0,1:T(2,128)(2,1)}), bf16[2,224,1024]{2,0,1:T(2,128)(2,1)S(1)}, u32[]{:S(2)}, u32[]{:S(2)}) async-start(bf16[2,224,1024]{2,0,1:T(2,128)(2,1)} %copy.112), calls=%async_computation.6 | async-start | bytes 1835008 | tf_op jit(solution)/shard_map/all_to_all | solution.py:103
  165.8 24.1 %all-to-all-start.7 = ((bf16[2,224,1024]{2,0,1:T(2,128)(2,1)}), bf16[2,224,1024]{2,0,1:T(2,128)(2,1)S(1)}, u32[]{:S(2)}, u32[]{:S(2)}) async-start(bf16[2,224,1024]{2,0,1:T(2,128)(2,1)} %copy.114), calls=%async_computation.7 | async-start | bytes 1835008 | tf_op jit(solution)/shard_map/all_to_all | solution.py:106
  191.5 17.5 %copy-start.7 = (bf16[224,1024]{1,0:T(8,128)(2,1)S(1)}, bf16[224,1024]{1,0:T(8,128)(2,1)}, u32[]{:S(2)}) copy-start(bf16[224,1024]{1,0:T(8,128)(2,1)} %param.19) | copy-start | bytes 1376260
  216.0 202.7 %all-to-all-start.9 = ((bf16[32,224,1024]{2,1,0:T(8,128)(2,1)}), bf16[32,224,1024]{2,1,0:T(8,128)(2,1)}, u32[]{:S(2)}, u32[]{:S(2)}) async-start(bf16[32,224,1024]{2,1,0:T(8,128)(2,1)} %stack.2), calls=%async_computation.9 | async-start | bytes 29360128 | tf_op jit(solution)/shard_map/all_to_all | solution.py:159
  221.1 1.0 copy-start.6
  221.2 499.0 %reduce-scatter.2.cloned.1.call-start = ((), (), s32[]{:S(2)}) async-start(), calls=%async_computation.12 | async-start | bytes 2293760 | tf_op jit(solution)/shard_map/reduce_scatter | solution.py:196
  537.5 182.7 %copy-start.1 = (bf16[224,1024]{1,0:T(8,128)(2,1)S(1)}, bf16[224,1024]{1,0:T(8,128)(2,1)}, u32[]{:S(2)}) copy-start(bf16[224,1024]{1,0:T(8,128)(2,1)} %param.17) | copy-start | bytes 1376260
Sparse Core Ops, SparseCore 0:
  10.4 178.2 all-gather.1
  545.5 174.5 reduce-scatter.1
